TPU v7x, 512 devices: a whole 4x4x16 slice. The times are simulated.
512 devices in a mesh: seq: 64 (over x, z), head: 8 (over y, core).
Axes of the slice: x: 4, y: 4, z: 16, core: 2. Of those that a mesh axis runs over, the one named last changes fastest.
Arguments:
- queries: bfloat16 [8192, 4096], P('seq', 'head'), may hold values from -6 to 6
- keys: bfloat16 [8192, 4096], P('seq', 'head'), may hold values from -6 to 6
- values: bfloat16 [8192, 4096], P('seq', 'head'), may hold values from -6 to 6
- log_decay: float32 [8192, 32], P('seq', 'head'), may hold values from -0.75 to 0
- norm_gain: float32 [4096], P('head'), may hold values from 0.1 to 1.9
- out_weight: bfloat16 [4096, 4096], P('head'), may hold values from -0.125 to 0.125
- steer_ids: int32 [8192], P('seq'), may hold values from 0 to 15
- steer_table: bfloat16 [16, 4096], P(None, 'head'), may hold values from -3 to 3
Outputs:
- layer_out: bfloat16 [8192, 4096], P('seq', 'head')
All inputs are finite; a program needn't handle non-finite values.
Results may differ from a plain program's by a relative error of at most 0.0052.
Values sent between devices are 32-bit elements; how exact they have to be, the bound alone decides.
No kernel may reach another device: no remote copies, remote signals or barrier semaphores. Data moves between devices by JAX's collectives and lax.ppermute only.
A program may use at most 64 MiB of HBM per device.

v0:
```python
import jax
import jax.numpy as jnp
from jax import lax
from jax.sharding import PartitionSpec as P

SPAN = 128


def prefix(part, axis, combine, identity):
    place = lax.axis_index(axis)
    gathered = jax.tree.map(lambda a: lax.all_gather(a, axis), part)
    state = jax.tree.map(lambda a, e: jnp.zeros_like(a) + jnp.asarray(e, a.dtype), part, identity)

    def one(step, state):
        return combine(
            state, jax.tree.map(lambda a: lax.dynamic_index_in_dim(a, step, 0, False), gathered)
        )

    return lax.fori_loop(0, place, one, state)


def block_step(state, inputs):
    query, key_blk, value_blk, decay = inputs
    cum = jnp.cumsum(decay, axis=1)
    size = decay.shape[1]
    rows = lax.broadcasted_iota(jnp.int32, (size, size), 0)
    cols = lax.broadcasted_iota(jnp.int32, (size, size), 1)
    lower = (cols <= rows)[None]
    scores = jnp.einsum("hte,hse->hts", query, key_blk, preferred_element_type=jnp.float32)
    diffs = jnp.where(lower, cum[:, :, None] - cum[:, None, :], 0.0)
    block_weights = (jnp.where(lower, jnp.exp(diffs), 0.0) * scores).astype(jnp.bfloat16)
    intra = jnp.einsum("hts,hse->hte", block_weights, value_blk, preferred_element_type=jnp.float32)
    inter = jnp.exp(cum)[:, :, None] * jnp.einsum(
        "hte,hef->htf", query.astype(jnp.float32), state, precision=lax.Precision.HIGHEST
    )
    total = cum[:, -1]
    scaled_keys = key_blk.astype(jnp.float32) * jnp.exp(total[:, None] - cum)[:, :, None]
    update = jnp.einsum(
        "hse,hsf->hef", scaled_keys, value_blk.astype(jnp.float32), precision=lax.Precision.HIGHEST
    )
    new_state = jnp.exp(total)[:, None, None] * state + update
    return (new_state, intra + inter)


def join_memory(earlier, later):
    return (earlier[0] + later[0], jnp.exp(later[0])[:, None, None] * earlier[1] + later[1])


def shards(queries, keys, values, log_decay, norm_gain, out_weight, steer_ids, steer_table):
    tok_rows, features = queries.shape
    heads_here = log_decay.shape[1]
    head_size = features // heads_here
    count = tok_rows // SPAN

    def split(array):
        return array.reshape(count, SPAN, heads_here, head_size).transpose(0, 2, 1, 3)

    decays = log_decay.reshape(count, SPAN, heads_here).transpose(0, 2, 1)
    start = jnp.zeros((heads_here, head_size, head_size), jnp.float32)
    local_memory, blocks = lax.scan(
        block_step, start, (split(queries), split(keys), split(values), decays)
    )
    device_log = jnp.sum(log_decay, axis=0)
    identity = (jnp.zeros((heads_here,), jnp.float32), start)
    passed = prefix((device_log, local_memory), "seq", join_memory, identity)
    earlier_memory = passed[1]
    running = jnp.cumsum(log_decay, axis=0)
    query_heads = queries.reshape(tok_rows, heads_here, head_size).astype(jnp.float32)
    carried = jnp.exp(running)[:, :, None] * jnp.einsum(
        "the,hef->thf", query_heads, earlier_memory, precision=lax.Precision.HIGHEST
    )
    attended = blocks.transpose(0, 2, 1, 3).reshape(tok_rows, heads_here, head_size) + carried
    mean_sq = jnp.mean(attended * attended, axis=-1, keepdims=True)
    normed = (attended * lax.rsqrt(mean_sq + 1e-06)).reshape(tok_rows, features) * norm_gain
    normed = normed.astype(jnp.bfloat16)
    partial_term = jnp.dot(normed, out_weight, preferred_element_type=jnp.float32)
    onehot = (
        steer_ids[:, None] == jnp.arange(steer_table.shape[0], dtype=jnp.int32)[None, :]
    ).astype(jnp.bfloat16)
    steering = jnp.dot(onehot, steer_table, preferred_element_type=jnp.float32)
    whole_sum = lax.psum(partial_term, "head")
    column_width = steer_table.shape[1]
    summed = lax.dynamic_slice_in_dim(
        whole_sum, lax.axis_index("head") * column_width, column_width, 1
    )
    return (summed + steering).astype(jnp.bfloat16)


def solution(mesh):
    in_specs = (
        P("seq", "head"),
        P("seq", "head"),
        P("seq", "head"),
        P("seq", "head"),
        P("head"),
        P("head", None),
        P("seq"),
        P(None, "head"),
    )
    out_specs = P("seq", "head")
    return jax.shard_map(shards, mesh=mesh, in_specs=in_specs, out_specs=out_specs, check_vma=False)
```

profile of v0, /device:TPU:2, one launch (start us, length us, event | category | flops | bytes accessed | tf_op | source)
XLA Modules:
  0.0 363.3 jit_solution(9025703200872860775)
XLA Ops:
  6.5 0.0 copy-start
  6.5 0.0 all-gather.4.cloned.1.call-start
  6.5 1.0 reduce_window_sum.23
  7.6 0.2 slice_reduce_fusion
  7.7 0.1 subtract_exponential_fusion
  7.8 1.0 copy.41
  8.9 0.9 reshape.85
  9.8 1.0 convolution_add_fusion
  10.8 0.0 all-gather.4.cloned.1.call-update
  10.8 0.0 all-reduce.3.cloned.1.call-start
  10.9 0.8 reduce_sum.18
  11.7 0.8 copy.33
  12.4 0.9 reshape.83
  13.4 1.3 dynamic-slice.5
  15.4 0.2 dynamic-update-slice
  15.6 129.7 %all-reduce = f32[256]{0:T(256)S(1)} all-reduce(f32[256]{0:T(256)S(1)} %dynamic-update-slice), channel_id=2, replica_groups=mesh['seq'=64,'head'=8] {'seq'}, use_global_device_ids=true, to_apply=%add | all-reduce | flops 256 | bytes 2048
  145.3 0.1 reshape.89
  145.5 0.2 reduce_window_sum.24
  145.7 0.1 copy.34
  145.8 0.4 fusion.7
  146.1 0.4 fusion.4
  146.5 61.4 %all-gather.4.cloned.1.call-done = f32[256,128,128]{2,1,0:T(8,128)} async-done(((f32[4,128,128]{2,1,0:T(8,128)}), f32[256,128,128]{2,1,0:T(8,128)}) %all-gather.4.cloned.1.call-update) | async-done | bytes 16777232 | tf_op jit(solution)/shard_map/all_gather | solution.py:11
  207.9 17.7 %while.3 = (s32[]{:T(128)}, f32[4,128,128]{2,1,0:T(8,128)S(1)}, s32[]{:T(128)}, f32[64,4]{1,0:T(8,128)S(1)}, f32[64,4,128,128]{3,2,1,0:T(8,128)}, /*index=5*/s32[]{:T(128)}, s32[]{:T(128)}, s32[]{:T(128)}) while((s32[]{:T(128)}, f32[4,128,128]{2,1,0:T(8,128)S(1)}, s32[]{:T(128)}, f32[64,4]{1,0:T(8,128)S(1)}, f32[64,4,128,128]{3,2,1,0:T(8,128)}, ...), condition=%wide.region_4.5_spmd, body=%wide.region_3.4_spmd.sunk | while | flops 131077 | bytes 786615 | solution.py:19
  207.9 1.1 bitcast_add_fusion.2
  209.0 1.1 bitcast_add_fusion.2
  210.1 1.1 bitcast_add_fusion.2
  211.2 1.1 bitcast_add_fusion.2
  212.4 1.1 bitcast_add_fusion.2
  213.5 1.1 bitcast_add_fusion.2
  214.6 1.1 bitcast_add_fusion.2
  215.7 1.1 bitcast_add_fusion.2
  216.8 1.1 bitcast_add_fusion.2
  217.9 1.1 bitcast_add_fusion.2
  219.0 1.1 bitcast_add_fusion.2
  220.1 1.1 bitcast_add_fusion.2
  221.2 1.1 bitcast_add_fusion.2
  222.3 1.1 bitcast_add_fusion.2
  223.4 1.1 bitcast_add_fusion.2
  224.5 1.1 bitcast_add_fusion.2
  225.6 0.0 copy-done.1
  225.6 0.4 multiply_reduce_fusion
  226.0 0.0 copy-done.2
  226.0 0.1 fusion.8
  226.2 0.0 copy-start.3
  226.2 4.2 %fusion.36 = f32[128,4096]{1,0:T(8,128)} fusion(bf16[128,512]{0,1:T(8,128)(2,1)S(1)} %fusion.8, bf16[512,4096]{1,0:T(8,128)(2,1)} %param.15), kind=kOutput, calls=%fused_computation.50 | convolution fusion | flops 536870912 | bytes 6422528 | tf_op jit(solution)/shard_map/dot_general | solution.py:76
  230.4 0.0 all-reduce.3.cloned.1.call-update
  230.5 124.1 %all-reduce.3.cloned.1.call-done = f32[128,4096]{1,0:T(8,128)} async-done(((f32[128,4096]{1,0:T(8,128)}), f32[128,4096]{1,0:T(8,128)}) %all-reduce.3.cloned.1.call-update) | async-done | bytes 2097168 | tf_op jit(solution)/shard_map/psum | solution.py:81
  354.6 1.8 fusion.6
  (27 shorter events, 0.3 us)
Async XLA Ops:
  6.5 348.1 %copy-start = (bf16[16,512]{1,0:T(8,128)(2,1)S(1)}, bf16[16,512]{1,0:T(8,128)(2,1)}, u32[]{:S(2)}) copy-start(bf16[16,512]{1,0:T(8,128)(2,1)} %param.17) | copy-start | bytes 49156
  6.5 219.0 %copy-start.1 = (bf16[128,512]{1,0:T(8,128)(2,1)S(1)}, bf16[128,512]{1,0:T(8,128)(2,1)}, u32[]{:S(2)}) copy-start(bf16[128,512]{1,0:T(8,128)(2,1)} %param.10) | copy-start | bytes 393220
  6.5 201.3 %all-gather.4.cloned.1.call-start = ((), (), s32[]{:S(2)}) async-start(), calls=%async_computation.1 | async-start | bytes 17039360 | tf_op jit(solution)/shard_map/all_gather | solution.py:11
  10.8 215.3 %copy-start.2 = (f32[512]{0:T(512)S(1)}, f32[512]{0:T(512)}, u32[]{:S(2)}) copy-start(f32[512]{0:T(512)} %param.14) | copy-start | bytes 6148
  10.8 343.8 %all-reduce.3.cloned.1.call-start = ((), (), s32[]{:S(2)}) async-start(), calls=%async_computation | async-start | bytes 4194304 | tf_op jit(solution)/shard_map/psum | solution.py:81
  226.2 128.4 %copy-start.3 = (s32[128]{0:T(128)S(1)}, s32[128]{0:T(128)}, u32[]{:S(2)}) copy-start(s32[128]{0:T(128)} %param.16) | copy-start | bytes 1540
Sparse Core Ops, SparseCore 0:
  10.9 196.8 all-gather.3
  230.6 123.9 all-reduce.2
where the time goes:
time: 366 us; the launch traced here: 363 us
  waiting for transfers between devices  186 us (51%)
  blocking collectives  130 us (36%)
  other arithmetic  19.2 us (5%)
  between operations  14.2 us (4%)
  matrix products  8.18 us (2%)
  local copies, waits for them, and re-layouts  5.91 us (2%)
    unnamed x1, blocking collectives  130 us
    psum x1, waiting for transfers between devices, shards(): whole_sum = lax.psum(partial_term, 'head')  124 us
    all_gather x1, waiting for transfers between devices, prefix(): gathered = jax.tree.map(lambda a: lax.all_gather(a, axis), part)  61.4 us
    add x16, other arithmetic, join_memory(): jnp.exp(later[0])[:, None, None] * earlier[1] + later[1]  17 us
  transfers between devices with their start and end apart: 2, of which 2 were waited for; matrix products, arithmetic and copies ran while one was open for 1% of the time, Pallas kernels for 0%

commit v1 on v0

--- a/solution.py
+++ b/solution.py
@@ -78,7 +78,11 @@
         steer_ids[:, None] == jnp.arange(steer_table.shape[0], dtype=jnp.int32)[None, :]
     ).astype(jnp.bfloat16)
     steering = jnp.dot(onehot, steer_table, preferred_element_type=jnp.float32)
-    whole_sum = lax.psum(partial_term, "head")
+    whole_sum = partial_term
+    for hop in (1, 2, 4):
+        whole_sum = whole_sum + lax.ppermute(
+            whole_sum, "head", [(dev, dev ^ hop) for dev in range(8)]
+        )
     column_width = steer_table.shape[1]
     summed = lax.dynamic_slice_in_dim(
         whole_sum, lax.axis_index("head") * column_width, column_width, 1

time: 366 us -> 390 us (1.066)
  the two profiles are of different devices: /device:TPU:2 before, /device:TPU:486 now
where the time goes in v1:
time: 390 us; the launch traced here: 387 us
  waiting for transfers between devices  139 us (36%)
  blocking collectives  139 us (36%)
  other arithmetic  69.6 us (18%)
  between operations  14.2 us (4%)
  starting transfers between devices  10.2 us (3%)
  matrix products  6.88 us (2%)
  local copies, waits for them, and re-layouts  6.45 us (2%)
    unnamed x1, blocking collectives  139 us
    ppermute x3, waiting for transfers between devices, shards(): lax.ppermute(whole_sum, 'head', [(dev, dev ^ hop) for dev in range(8)])  95.7 us
    add x63, other arithmetic, join_memory(): jnp.exp(later[0])[:, None, None] * earlier[1] + later[1]  66.9 us
    all_gather x1, waiting for transfers between devices, prefix(): gathered = jax.tree.map(lambda a: lax.all_gather(a, axis), part)  43.1 us
    ppermute x3, starting transfers between devices, shards(): lax.ppermute(whole_sum, 'head', [(dev, dev ^ hop) for dev in range(8)])  10.2 us
  transfers between devices with their start and end apart: 4, of which 4 were waited for; matrix products, arithmetic and copies ran while one was open for 1% of the time, Pallas kernels for 0%

profile of v1, /device:TPU:486, one launch (start us, length us, event | category | flops | bytes accessed | tf_op | source)
XLA Modules:
  0.0 387.3 jit_solution(2469084908864610987)
XLA Ops:
  13.3 1.3 dynamic-slice.5
  15.5 139.3 %all-reduce = f32[256]{0:T(256)S(1)} all-reduce(f32[256]{0:T(256)S(1)} %dynamic-update-slice), channel_id=2, replica_groups=mesh['seq'=64,'head'=8] {'seq'}, use_global_device_ids=true, to_apply=%add | all-reduce | flops 256 | bytes 2048
  156.0 43.1 %all-gather.4.cloned.1.call-done = f32[256,128,128]{2,1,0:T(8,128)} async-done(((f32[4,128,128]{2,1,0:T(8,128)}), f32[256,128,128]{2,1,0:T(8,128)}) %all-gather.4.cloned.1.call-update) | async-done | bytes 16777232 | tf_op jit(solution)/shard_map/all_gather | solution.py:11
  199.1 69.5 %while.3 = (s32[]{:T(128)}, f32[4,128,128]{2,1,0:T(8,128)S(1)}, s32[]{:T(128)}, f32[64,4]{1,0:T(8,128)S(1)}, f32[64,4,128,128]{3,2,1,0:T(8,128)}, /*index=5*/s32[]{:T(128)}, s32[]{:T(128)}, s32[]{:T(128)}) while((s32[]{:T(128)}, f32[4,128,128]{2,1,0:T(8,128)S(1)}, s32[]{:T(128)}, f32[64,4]{1,0:T(8,128)S(1)}, f32[64,4,128,128]{3,2,1,0:T(8,128)}, ...), condition=%wide.region_4.5_spmd, body=%wide.region_3.4_spmd.sunk | while | flops 131077 | bytes 786615 | solution.py:19
  199.2 1.1 bitcast_add_fusion.2
  200.3 1.1 bitcast_add_fusion.2
  201.4 1.1 bitcast_add_fusion.2
  202.5 1.1 bitcast_add_fusion.2
  203.6 1.1 bitcast_add_fusion.2
  204.7 1.1 bitcast_add_fusion.2
  205.8 1.1 bitcast_add_fusion.2
  206.9 1.1 bitcast_add_fusion.2
  208.0 1.1 bitcast_add_fusion.2
  209.1 1.1 bitcast_add_fusion.2
  210.2 1.1 bitcast_add_fusion.2
  211.3 1.1 bitcast_add_fusion.2
  212.4 1.1 bitcast_add_fusion.2
  213.5 1.1 bitcast_add_fusion.2
  214.6 1.1 bitcast_add_fusion.2
  215.7 1.1 bitcast_add_fusion.2
  216.8 1.1 bitcast_add_fusion.2
  217.9 1.1 bitcast_add_fusion.2
  219.0 1.1 bitcast_add_fusion.2
  221.2 1.1 bitcast_add_fusion.2
  222.3 1.1 bitcast_add_fusion.2
  223.5 1.1 bitcast_add_fusion.2
  224.6 1.1 bitcast_add_fusion.2
  225.7 1.1 bitcast_add_fusion.2
  226.8 1.1 bitcast_add_fusion.2
  227.9 1.1 bitcast_add_fusion.2
  229.0 1.1 bitcast_add_fusion.2
  230.1 1.1 bitcast_add_fusion.2
  231.2 1.1 bitcast_add_fusion.2
  232.3 1.1 bitcast_add_fusion.2
  233.4 1.1 bitcast_add_fusion.2
  234.5 1.1 bitcast_add_fusion.2
  235.6 1.1 bitcast_add_fusion.2
  236.7 1.1 bitcast_add_fusion.2
  237.8 1.1 bitcast_add_fusion.2
  238.9 1.1 bitcast_add_fusion.2
  269.3 2.9 fusion.38
  272.2 1.9 collective-permute-start
  274.1 4.1 %collective-permute-done = f32[128,4096]{1,0:T(8,128)S(1)} collective-permute-done((f32[128,4096]{1,0:T(8,128)S(1)}, f32[128,4096]{1,0:T(8,128)S(1)}, u32[]{:S(2)}, u32[]{:S(2)}) %collective-permute-start) | collective-permute-done | bytes 2097184 | tf_op jit(solution)/shard_map/ppermute | solution.py:83
  278.5 3.4 collective-permute-start.1
  281.9 46.2 %collective-permute-done.1 = f32[128,4096]{1,0:T(8,128)S(1)} collective-permute-done((f32[128,4096]{1,0:T(8,128)S(1)}, f32[128,4096]{1,0:T(8,128)S(1)}, u32[]{:S(2)}, u32[]{:S(2)}) %collective-permute-start.1) | collective-permute-done | bytes 2097184 | tf_op jit(solution)/shard_map/ppermute | solution.py:83
  328.3 4.9 %collective-permute-start.2 = (f32[128,4096]{1,0:T(8,128)S(1)}, f32[128,4096]{1,0:T(8,128)}, u32[]{:S(2)}, u32[]{:S(2)}) collective-permute-start(f32[128,4096]{1,0:T(8,128)S(1)} %add.61), channel_id=1, source_target_pairs={{0,4},{1,5},{2,6},{3,7},{4,0},{5,1},{6,2},{7,3},{8,12},{9,13},{10,... | collective-permute-start | bytes 6291464 | tf_op jit(solution)/shard_map/ppermute | solution.py:83
  333.3 45.4 %collective-permute-done.2 = f32[128,4096]{1,0:T(8,128)} collective-permute-done((f32[128,4096]{1,0:T(8,128)S(1)}, f32[128,4096]{1,0:T(8,128)}, u32[]{:S(2)}, u32[]{:S(2)}) %collective-permute-start.2) | collective-permute-done | bytes 2097184 | tf_op jit(solution)/shard_map/ppermute | solution.py:83
  378.7 1.8 fusion.8
  (126 shorter events, 38.6 us)
Async XLA Ops:
  6.5 372.1 %copy-start = (bf16[16,512]{1,0:T(8,128)(2,1)S(1)}, bf16[16,512]{1,0:T(8,128)(2,1)}, u32[]{:S(2)}) copy-start(bf16[16,512]{1,0:T(8,128)(2,1)} %param.17) | copy-start | bytes 49156
  6.5 192.5 %all-gather.4.cloned.1.call-start = ((), (), s32[]{:S(2)}) async-start(), calls=%async_computation | async-start | bytes 17039360 | tf_op jit(solution)/shard_map/all_gather | solution.py:11
  199.1 69.5 %copy-start.1 = (bf16[128,512]{1,0:T(8,128)(2,1)S(1)}, bf16[128,512]{1,0:T(8,128)(2,1)}, u32[]{:S(2)}) copy-start(bf16[128,512]{1,0:T(8,128)(2,1)} %param.10) | copy-start | bytes 393220
  199.1 70.0 %copy-start.2 = (f32[512]{0:T(512)S(1)}, f32[512]{0:T(512)}, u32[]{:S(2)}) copy-start(f32[512]{0:T(512)} %param.14) | copy-start | bytes 6148
  272.2 6.1 %collective-permute-start = (f32[128,4096]{1,0:T(8,128)S(1)}, f32[128,4096]{1,0:T(8,128)S(1)}, u32[]{:S(2)}, u32[]{:S(2)}) collective-permute-start(f32[128,4096]{1,0:T(8,128)S(1)} %fusion.38), channel_id=1, source_target_pairs={{0,1},{1,0},{2,3},{3,2},{4,5},{5,4},{6,7},{7,6},{8,9},{9,8},{10,11... | collective-permute-start | bytes 6291464 | tf_op jit(solution)/shard_map/ppermute | solution.py:83
  278.5 100.1 %copy-start.3 = (s32[128]{0:T(128)S(1)}, s32[128]{0:T(128)}, u32[]{:S(2)}) copy-start(s32[128]{0:T(128)} %param.16) | copy-start | bytes 1540
  278.5 49.6 %collective-permute-start.1 = (f32[128,4096]{1,0:T(8,128)S(1)}, f32[128,4096]{1,0:T(8,128)S(1)}, u32[]{:S(2)}, u32[]{:S(2)}) collective-permute-start(f32[128,4096]{1,0:T(8,128)S(1)} %add.60), channel_id=1, source_target_pairs={{0,2},{1,3},{2,0},{3,1},{4,6},{5,7},{6,4},{7,5},{8,10},{9,11},{10,... | collective-permute-start | bytes 6291464 | tf_op jit(solution)/shard_map/ppermute | solution.py:83
  328.3 50.3 %collective-permute-start.2 = (f32[128,4096]{1,0:T(8,128)S(1)}, f32[128,4096]{1,0:T(8,128)}, u32[]{:S(2)}, u32[]{:S(2)}) collective-permute-start(f32[128,4096]{1,0:T(8,128)S(1)} %add.61), channel_id=1, source_target_pairs={{0,4},{1,5},{2,6},{3,7},{4,0},{5,1},{6,2},{7,3},{8,12},{9,13},{10,... | collective-permute-start | bytes 6291464 | tf_op jit(solution)/shard_map/ppermute | solution.py:83
Sparse Core Ops, SparseCore 0:
  10.9 188.1 all-gather.3
